TPU v7x, 32 devices: a whole 2x2x4 slice. The times are simulated.
32 devices in a mesh: ctx: 8 (over z, y), dp: 2 (over x), section: 2 (over core).
Axes of the slice: x: 2, y: 2, z: 4, core: 2. Of those that a mesh axis runs over, the one named last changes fastest.
Arguments:
- normed: bfloat16 [2, 3072, 1024], P('dp', 'ctx'), may hold values from -40 to 40
- w_query: bfloat16 [1024, 1024], P('dp', 'section'), may hold values from -0.1875 to 0.1875
- w_key: bfloat16 [1024, 1024], P('dp', 'section'), may hold values from -0.28125 to 0.28125
- w_value: bfloat16 [1024, 1024], P('dp', 'section'), may hold values from -0.1875 to 0.1875
- block_mask: int32 [24, 7], replicated, may hold values from 0 to 1, as said below
- cotangent: bfloat16 [2, 3072, 1024], P('dp', 'ctx', 'section'), may hold values from -8 to 8
Outputs:
- attended: bfloat16 [2, 3072, 1024], P('dp', 'ctx', 'section')
- grad_input: bfloat16 [2, 3072, 1024], P('dp', 'ctx')
- grad_weights: float32 [1024, 3, 1024], P(('ctx', 'dp'), None, 'section')
Inputs may be any that keep to these rules, and one draw needn't show every extreme that they name: `block_mask`: every row has a 1 in column 3; no row names a key block outside 0 to 23; a row holds at most 5 ones, and some row holds exactly 5.
All inputs are finite; a program needn't handle non-finite values.
Results may differ from a plain program's by a relative error of at most 0.014.
The roundings to bfloat16 on the way count: a program that leaves them out, or rounds other values in their place, can miss the bound.
Values may be sent and summed in bfloat16 or wider, within the bound.
No kernel may reach another device: no remote copies, remote signals or barrier semaphores. Data moves between devices by JAX's collectives and lax.ppermute only.
A program may use at most 64 MiB of HBM per device.

v0:
```python
import jax
import jax.numpy as jnp
from jax import lax
from jax.sharding import PartitionSpec as P

HD = 64
BLOCK = 128
REACH = 3


def extended(cells, sides, width):
    for axis, dim in sides:
        count = lax.axis_size(axis)
        ends = count - 1
        head = lax.slice_in_dim(cells, 0, width, axis=dim)
        tail = lax.slice_in_dim(cells, cells.shape[dim] - width, cells.shape[dim], axis=dim)
        cells = jnp.concatenate(
            [
                lax.ppermute(tail, axis, [(i, (i + 1) % count) for i in range(ends)]),
                cells,
                lax.ppermute(head, axis, [((i + 1) % count, i) for i in range(ends)]),
            ],
            axis=dim,
        )
    return cells


def shifted(value, axis, steps):
    count = lax.axis_size(axis)
    leading, last = (max(0, -steps), min(count, count - steps))
    return lax.ppermute(value, axis, [(source, source + steps) for source in range(leading, last)])


def attend(query_block, key_window, seen_slots, score_scale):
    scores = (
        jnp.einsum("qhd,skhd->hqsk", query_block, key_window, preferred_element_type=jnp.float32)
        * score_scale
    )
    is_seen = seen_slots[None, None, :, None] > 0
    row_top = jnp.max(jnp.where(is_seen, scores, -jnp.inf), axis=(2, 3), keepdims=True)
    raised = jnp.where(is_seen, jnp.exp(scores - row_top), 0.0)
    row_total = jnp.sum(raised, axis=(2, 3), keepdims=True)
    return (raised / row_total, row_top, row_total)


def per_device(normed, w_query, w_key, w_value, block_mask, cotangent):
    tokens = normed[0]
    upstream = cotangent[0]
    length = tokens.shape[0]
    features = upstream.shape[1]
    head_count = features // HD
    blocks = length // BLOCK
    frame_len = blocks + 2 * REACH
    span_len = 2 * REACH + 1
    score_scale = HD ** (-0.5)
    query_full, key_full, value_full = (
        lax.all_gather(w_query, "dp", axis=0, tiled=True),
        lax.all_gather(w_key, "dp", axis=0, tiled=True),
        lax.all_gather(w_value, "dp", axis=0, tiled=True),
    )
    queries = jnp.dot(tokens, query_full, preferred_element_type=jnp.float32).astype(jnp.bfloat16)
    key_rows = jnp.dot(tokens, key_full, preferred_element_type=jnp.float32).astype(jnp.bfloat16)
    value_rows = jnp.dot(tokens, value_full, preferred_element_type=jnp.float32).astype(
        jnp.bfloat16
    )
    framed = extended(jnp.stack([key_rows, value_rows]), (("ctx", 1),), REACH * BLOCK)
    framed = framed.reshape(2, frame_len, BLOCK, head_count, HD)
    query_blocks = queries.reshape(blocks, BLOCK, head_count, HD)
    upstream_blocks = upstream.reshape(blocks, BLOCK, head_count, HD)
    first_block = lax.axis_index("ctx") * blocks
    padded_mask = jnp.pad(block_mask, ((REACH, REACH), (0, 0)))
    frame_mask = lax.dynamic_slice(padded_mask, (first_block, 0), (frame_len, span_len))
    own_mask = frame_mask[REACH : REACH + blocks]
    positions = jnp.arange(span_len, dtype=jnp.int32)
    slot_order = jnp.broadcast_to(positions[None, :], (blocks, span_len))
    slot_index = slot_order + jnp.arange(blocks, dtype=jnp.int32)[:, None]

    def windows(block_at):
        picked = lax.dynamic_slice_in_dim(framed, block_at, span_len, 1)
        return (picked[0], picked[1])

    def forward(running, block_at):
        query_block = lax.dynamic_index_in_dim(query_blocks, block_at, 0, False)
        key_window, value_window = windows(block_at)
        seen_slots = lax.dynamic_index_in_dim(own_mask, block_at, 0, False)
        probability, row_top, row_total = attend(query_block, key_window, seen_slots, score_scale)
        mixed_out = jnp.einsum(
            "hqsk,skhd->qhd",
            probability.astype(jnp.bfloat16),
            value_window,
            preferred_element_type=jnp.float32,
        ).astype(jnp.bfloat16)
        return (running, (mixed_out, row_top[:, :, 0, 0], row_total[:, :, 0, 0]))

    block_ids = jnp.arange(blocks, dtype=jnp.int32)
    _, (mixed_outs, row_tops, row_totals) = lax.scan(forward, jnp.zeros((), jnp.float32), block_ids)
    attended = mixed_outs.reshape(1, length, features)

    def backward(running, block_at):
        query_block = lax.dynamic_index_in_dim(query_blocks, block_at, 0, False)
        upstream_block = lax.dynamic_index_in_dim(upstream_blocks, block_at, 0, False)
        key_window, value_window = windows(block_at)
        seen_slots = lax.dynamic_index_in_dim(own_mask, block_at, 0, False)
        probability, _, _ = attend(query_block, key_window, seen_slots, score_scale)
        weights = probability.astype(jnp.bfloat16)
        prob_grad = jnp.einsum(
            "qhd,skhd->hqsk", upstream_block, value_window, preferred_element_type=jnp.float32
        )
        row_delta = jnp.sum(probability * prob_grad, axis=(2, 3), keepdims=True)
        score_grad = (probability * (prob_grad - row_delta)).astype(jnp.bfloat16)
        query_grad = (
            score_scale
            * jnp.einsum(
                "hqsk,skhd->qhd", score_grad, key_window, preferred_element_type=jnp.float32
            )
        ).astype(jnp.bfloat16)
        key_part = score_scale * jnp.einsum(
            "hqsk,qhd->skhd", score_grad, query_block, preferred_element_type=jnp.float32
        )
        value_part = jnp.einsum(
            "hqsk,qhd->skhd", weights, upstream_block, preferred_element_type=jnp.float32
        )
        slot_rows = lax.dynamic_index_in_dim(slot_index, block_at, 0, False)
        running = running.at[0, slot_rows].add(key_part).at[1, slot_rows].add(value_part)
        return (running, (query_grad, row_delta[:, :, 0, 0]))

    start_state = jnp.zeros((2, frame_len, BLOCK, head_count, HD), jnp.float32)
    frame_grads, (query_grads, row_deltas) = lax.scan(backward, start_state, block_ids)
    query_grad = query_grads.reshape(length, features)
    frame_grads = frame_grads.reshape(2, frame_len, BLOCK, features)
    left_side = frame_grads[:, :REACH]
    right_side = frame_grads[:, blocks + REACH :]
    middle = frame_grads[:, REACH : REACH + blocks]
    for offset in (1, -1):
        outgoing = right_side if offset == 1 else left_side
        arrived = shifted(outgoing.astype(jnp.bfloat16), "ctx", offset).astype(outgoing.dtype)
        if offset == 1:
            middle = middle.at[:, :REACH].add(arrived)
        else:
            middle = middle.at[:, blocks - REACH :].add(arrived)
    key_grad = middle[0].reshape(length, features).astype(jnp.bfloat16)
    value_grad = middle[1].reshape(length, features).astype(jnp.bfloat16)
    contract = (((1,), (1,)), ((), ()))
    partial_input = (
        lax.dot_general(query_grad, query_full, contract, preferred_element_type=jnp.float32)
        + lax.dot_general(key_grad, key_full, contract, preferred_element_type=jnp.float32)
        + lax.dot_general(value_grad, value_full, contract, preferred_element_type=jnp.float32)
    )
    grad_input = lax.psum(partial_input.astype(jnp.bfloat16), "section")[None]
    grads_all = jnp.stack([query_grad, key_grad, value_grad], axis=1)
    group_part = lax.psum_scatter(
        jnp.einsum("tr,tcf->rcf", tokens, grads_all, preferred_element_type=jnp.float32).astype(
            jnp.bfloat16
        ),
        "ctx",
        scatter_dimension=0,
        tiled=True,
    )
    summed = lax.psum_scatter(group_part, "dp", scatter_dimension=0, tiled=True).astype(jnp.float32)
    grad_weights = summed / lax.axis_size("dp")
    return (attended, grad_input, grad_weights)


def solution(mesh):
    in_specs = (
        P("dp", "ctx", None),
        P("dp", "section"),
        P("dp", "section"),
        P("dp", "section"),
        P(),
        P("dp", "ctx", "section"),
    )
    out_specs = (P("dp", "ctx", "section"), P("dp", "ctx", None), P(("ctx", "dp"), None, "section"))
    return jax.shard_map(
        per_device, mesh=mesh, in_specs=in_specs, out_specs=out_specs, check_vma=False
    )
```

profile of v0, /device:TPU:0, one launch (start us, length us, event | category | flops | bytes accessed | tf_op | source)
XLA Modules:
  0.0 379.1 jit_solution(11920346828465409349)
XLA Ops:
  9.5 24.1 %all-gather.6.cloned.1.call-done = bf16[1024,512]{1,0:T(8,128)(2,1)} async-done(((bf16[512,512]{1,0:T(8,128)(2,1)}), bf16[1024,512]{1,0:T(8,128)(2,1)}) %all-gather.6.cloned.1.call-update) | async-done | bytes 1048592 | tf_op jit(solution)/shard_map/all_gather | solution.py:59
  35.4 21.1 %all-gather.4.cloned.1.call-done = bf16[1024,512]{1,0:T(8,128)(2,1)} async-done(((bf16[512,512]{1,0:T(8,128)(2,1)}), bf16[1024,512]{1,0:T(8,128)(2,1)}) %all-gather.4.cloned.1.call-update) | async-done | bytes 1048592 | tf_op jit(solution)/shard_map/all_gather | solution.py:58
  60.4 5.5 %collective-permute-start = (bf16[2,384,512]{2,1,0:T(8,128)(2,1)S(1)}, bf16[2,384,512]{2,1,0:T(8,128)(2,1)}, u32[]{:S(2)}, u32[]{:S(2)}) collective-permute-start(bf16[2,384,512]{2,1,0:T(8,128)(2,1)S(1)} %pad_maximum_fusion.1), channel_id=1, source_target_pairs={{0,4},{4,8},{8,12},{12,16},{16,20},{20,24},{24,28},{1,5},{5,9},{9,... | collective-permute-start | bytes 2359304 | tf_op jit(solution)/shard_map/ppermute | solution.py:19
  68.1 11.2 %all-gather.8.cloned.1.call-done = bf16[1024,512]{1,0:T(8,128)(2,1)} async-done(((bf16[512,512]{1,0:T(8,128)(2,1)}), bf16[1024,512]{1,0:T(8,128)(2,1)}) %all-gather.8.cloned.1.call-update) | async-done | bytes 1048592 | tf_op jit(solution)/shard_map/all_gather | solution.py:57
  82.9 14.1 %collective-permute-done = bf16[2,384,512]{2,1,0:T(8,128)(2,1)} collective-permute-done((bf16[2,384,512]{2,1,0:T(8,128)(2,1)S(1)}, bf16[2,384,512]{2,1,0:T(8,128)(2,1)}, u32[]{:S(2)}, u32[]{:S(2)}) %collective-permute-start) | collective-permute-done | bytes 786464 | tf_op jit(solution)/shard_map/ppermute | solution.py:19
  98.8 4.6 %reshape.200 = bf16[2,9,128,8,64]{4,3,2,1,0:T(8,128)(2,1)} reshape(bf16[2,1152,512]{2,1,0:T(8,128)(2,1)S(1)} %pad_maximum_fusion) | data formatting | bytes 4718592 | tf_op jit(solution)/shard_map/reshape | solution.py:67
  103.3 6.1 %copy.83 = bf16[2,9,128,8,64]{2,4,1,3,0:T(8,128)(2,1)} copy(bf16[2,9,128,8,64]{4,3,2,1,0:T(8,128)(2,1)} %reshape.200) | data formatting | bytes 4718592 | tf_op jit(solution)/shard_map/while | solution.py:96
  109.5 2.8 broadcast_in_dim.61
  112.3 76.9 %while.27 = (s32[]{:T(128)}, f32[2,9,128,8,64]{2,4,3,1,0:T(8,128)}, bf16[3,128,8,64]{1,3,2,0:T(8,128)(2,1)S(1)}, s32[3]{0:T(128)S(1)}, s32[3,7]{1,0:T(4,128)S(1)...) while((s32[]{:T(128)}, f32[2,9,128,8,64]{2,4,3,1,0:T(8,128)}, ...), condition=%wide.region_10.11_spmd, body=%wide.region_4.10_spmd.sunk | while | flops 611644544 | bytes 56669256 | solution.py:128
  121.1 2.6 multiply_reduce_fusion.2
  128.9 4.8 %scatter_fusion = f32[2,9,128,8,64]{2,4,3,1,0:T(8,128)} fusion(f32[2,9,128,8,64]{2,4,3,1,0:T(8,128)} %get-tuple-element.398, s32[7]{0:T(128)S(1)} %select_bitcast_fusion.5, f32[7,128,8,64]{1,3,2,0:T(8,128)} %copy.129), kind=kCustom, calls=%fused_computation.clone.1 | custom fusion | flops 458752 | bytes 5505080 | tf_op jit(solution)/shard_map/while/body/eval_jaxpr/scatter-add | solution.py:124
  133.7 4.3 %scatter_fusion.1 = f32[2,9,128,8,64]{2,4,3,1,0:T(8,128)} fusion(f32[2,9,128,8,64]{2,4,3,1,0:T(8,128)} %scatter_fusion, s32[7]{0:T(128)S(1)} %get-tuple-element.349, f32[7,128,8,64]{1,3,2,0:T(8,128)S(1)} %copy.130), kind=kCustom, calls=%fused_computation.1.clone.1 | custom fusion | flops 458752 | bytes 5505080 | tf_op jit(solution)/shard_map/while/body/eval_jaxpr/scatter-add | solution.py:124
  154.6 4.8 %scatter_fusion = f32[2,9,128,8,64]{2,4,3,1,0:T(8,128)} fusion(f32[2,9,128,8,64]{2,4,3,1,0:T(8,128)} %get-tuple-element.398, s32[7]{0:T(128)S(1)} %select_bitcast_fusion.5, f32[7,128,8,64]{1,3,2,0:T(8,128)} %copy.129), kind=kCustom, calls=%fused_computation.clone.1 | custom fusion | flops 458752 | bytes 5505080 | tf_op jit(solution)/shard_map/while/body/eval_jaxpr/scatter-add | solution.py:124
  159.4 4.2 %scatter_fusion.1 = f32[2,9,128,8,64]{2,4,3,1,0:T(8,128)} fusion(f32[2,9,128,8,64]{2,4,3,1,0:T(8,128)} %scatter_fusion, s32[7]{0:T(128)S(1)} %get-tuple-element.349, f32[7,128,8,64]{1,3,2,0:T(8,128)S(1)} %copy.130), kind=kCustom, calls=%fused_computation.1.clone.1 | custom fusion | flops 458752 | bytes 5505080 | tf_op jit(solution)/shard_map/while/body/eval_jaxpr/scatter-add | solution.py:124
  180.2 4.8 %scatter_fusion = f32[2,9,128,8,64]{2,4,3,1,0:T(8,128)} fusion(f32[2,9,128,8,64]{2,4,3,1,0:T(8,128)} %get-tuple-element.398, s32[7]{0:T(128)S(1)} %select_bitcast_fusion.5, f32[7,128,8,64]{1,3,2,0:T(8,128)} %copy.129), kind=kCustom, calls=%fused_computation.clone.1 | custom fusion | flops 458752 | bytes 5505080 | tf_op jit(solution)/shard_map/while/body/eval_jaxpr/scatter-add | solution.py:124
  185.0 4.2 %scatter_fusion.1 = f32[2,9,128,8,64]{2,4,3,1,0:T(8,128)} fusion(f32[2,9,128,8,64]{2,4,3,1,0:T(8,128)} %scatter_fusion, s32[7]{0:T(128)S(1)} %get-tuple-element.349, f32[7,128,8,64]{1,3,2,0:T(8,128)S(1)} %copy.130), kind=kCustom, calls=%fused_computation.1.clone.1 | custom fusion | flops 458752 | bytes 5505080 | tf_op jit(solution)/shard_map/while/body/eval_jaxpr/scatter-add | solution.py:124
  189.3 2.9 bitcast_convert_fusion
  192.3 5.4 %collective-permute-start.2 = (bf16[2,3,128,512]{2,3,1,0:T(8,128)(2,1)S(1)}, bf16[2,3,128,512]{2,3,1,0:T(8,128)(2,1)}, u32[]{:S(2)}, u32[]{:S(2)}) collective-permute-start(bf16[2,3,128,512]{2,3,1,0:T(8,128)(2,1)S(1)} %get-tuple-element.236), channel_id=1, source_target_pairs={{0,4},{4,8},{8,12},{12,16},{16,20},{20,24},{24,28},{1,5},{5,9},{9,... | collective-permute-start | bytes 2359304 | tf_op jit(solution)/shard_map/ppermute | solution.py:31
  201.6 29.0 %collective-permute-done.2 = bf16[2,3,128,512]{2,3,1,0:T(8,128)(2,1)} collective-permute-done((bf16[2,3,128,512]{2,3,1,0:T(8,128)(2,1)S(1)}, bf16[2,3,128,512]{2,3,1,0:T(8,128)(2,1)}, u32[]{:S(2)}, u32[]{:S(2)}) %collective-permute-start.2) | collective-permute-done | bytes 786464 | tf_op jit(solution)/shard_map/ppermute | solution.py:31
  233.7 4.5 %convolution_convert_fusion = bf16[3,512,1024]{2,1,0:T(8,128)(2,1)} fusion(bf16[384,1,512]{0,2,1:T(8,128)(2,1)S(1)} %copy.97, bf16[384,1,512]{0,2,1:T(8,128)(2,1)S(1)} %copy.96, bf16[384,1,512]{0,2,1:T(8,128)(2,1)} %stack_reshape.3, bf16[1,384,1024]{2,1,0:T(8,128)(2,1)S(1)} %copy-done), kind=kOutput, calls=%fused_computation.64 | convolution fusion | flops 1210712064 | bytes 5111808 | tf_op jit(solution)/shard_map/tr,tcf->rcf/dot_general | solution.py:152
  238.1 4.7 %copy.120 = bf16[1024,1536]{1,0:T(8,128)(2,1)} copy(bf16[1024,1536]{0,1:T(8,128)(2,1)} %bitcast.204) | data formatting | bytes 6291456
  246.0 71.7 %reduce-scatter.4.cloned.1.call-done = bf16[128,1536]{1,0:T(8,128)(2,1)} async-done(((bf16[1024,1536]{1,0:T(8,128)(2,1)}), bf16[128,1536]{1,0:T(8,128)(2,1)}) %reduce-scatter.4.cloned.1.call-update) | async-done | bytes 393232
  324.0 27.1 %while.26 = (s32[]{:T(128)}, bf16[3,128,8,64]{1,3,2,0:T(8,128)(2,1)S(1)}, s32[3]{0:T(128)S(1)}, bf16[2,9,128,8,64]{2,4,1,3,0:T(8,128)(2,1)}, s32[3,7]{1,0:T(4,12...) while((s32[]{:T(128)}, ...), condition=%wide.region_3.4_spmd, body=%wide.region_0.3_spmd.sunk | while | flops 245954576 | bytes 13128970 | solution.py:96
  354.7 15.5 %all-reduce.7.cloned.1.call-done = bf16[1,384,1024]{2,1,0:T(8,128)(2,1)} async-done(((bf16[1,384,1024]{2,1,0:T(8,128)(2,1)}), bf16[1,384,1024]{2,1,0:T(8,128)(2,1)}) %all-reduce.7.cloned.1.call-update) | async-done | bytes 786448 | tf_op jit(solution)/shard_map/psum | solution.py:149
  (131 shorter events, 91.4 us)
Async XLA Ops:
  7.2 26.4 %copy-start = (bf16[1,384,1024]{2,1,0:T(8,128)(2,1)S(1)}, bf16[1,384,1024]{2,1,0:T(8,128)(2,1)}, u32[]{:S(2)}) copy-start(bf16[1,384,1024]{2,1,0:T(8,128)(2,1)} %param.18) | copy-start | bytes 2359300
  7.2 26.4 %all-gather.6.cloned.1.call-start = ((), (), s32[]{:S(2)}) async-start(), calls=%async_computation.2 | async-start | bytes 1572864 | tf_op jit(solution)/shard_map/all_gather | solution.py:59
  7.9 48.6 %all-gather.4.cloned.1.call-start = ((), (), s32[]{:S(2)}) async-start(), calls=%async_computation.1 | async-start | bytes 1572864 | tf_op jit(solution)/shard_map/all_gather | solution.py:58
  8.7 57.2 %copy-start.10 = (s32[24,7]{0,1:T(8,128)S(1)}, s32[24,7]{0,1:T(8,128)}, u32[]{:S(2)}) copy-start(s32[24,7]{0,1:T(8,128)} %param.22) | copy-start | bytes 2020
  8.7 57.3 %copy-start.9 = (bf16[1,384,512]{2,1,0:T(8,128)(2,1)S(1)}, bf16[1,384,512]{2,1,0:T(8,128)(2,1)}, u32[]{:S(2)}) copy-start(bf16[1,384,512]{2,1,0:T(8,128)(2,1)} %param.23) | copy-start | bytes 1179652
  8.7 70.7 %all-gather.8.cloned.1.call-start = ((), (), s32[]{:S(2)}) async-start(), calls=%async_computation.3 | async-start | bytes 1572864 | tf_op jit(solution)/shard_map/all_gather | solution.py:57
  9.4 308.3 %reduce-scatter.4.cloned.1.call-start = ((), (), s32[]{:S(2)}) async-start(), calls=%async_computation.5 | async-start | bytes 3538944
  35.4 30.5 %copy-start.4 = (bf16[1,384,512]{2,1,0:T(8,128)(2,1)}, bf16[1,384,512]{2,1,0:T(8,128)(2,1)S(1)}, u32[]{:S(2)}) copy-start(bf16[1,384,512]{2,1,0:T(8,128)(2,1)S(1)} %fusion.44) | copy-start | bytes 1179652
  58.3 0.7 copy-start.5
  59.1 22.9 %collective-permute-start.1 = (bf16[2,384,512]{2,1,0:T(8,128)(2,1)S(1)}, bf16[2,384,512]{2,1,0:T(8,128)(2,1)S(1)}, u32[]{:S(2)}, u32[]{:S(2)}) collective-permute-start(bf16[2,384,512]{2,1,0:T(8,128)(2,1)S(1)} %pad_maximum_fusion.1), channel_id=1, source_target_pairs={{4,0},{8,4},{12,8},{16,12},{20,16},{24,20},{28,24},{5,1},{9,5},{13... | collective-permute-start | bytes 2359304 | tf_op jit(solution)/shard_map/ppermute | solution.py:21
  60.4 36.6 %collective-permute-start = (bf16[2,384,512]{2,1,0:T(8,128)(2,1)S(1)}, bf16[2,384,512]{2,1,0:T(8,128)(2,1)}, u32[]{:S(2)}, u32[]{:S(2)}) collective-permute-start(bf16[2,384,512]{2,1,0:T(8,128)(2,1)S(1)} %pad_maximum_fusion.1), channel_id=1, source_target_pairs={{0,4},{4,8},{8,12},{12,16},{16,20},{20,24},{24,28},{1,5},{5,9},{9,... | collective-permute-start | bytes 2359304 | tf_op jit(solution)/shard_map/ppermute | solution.py:19
  82.1 0.9 copy-start.8
  109.5 2.9 copy-start.11
  189.3 3.1 copy-start.6
  192.3 38.3 %collective-permute-start.2 = (bf16[2,3,128,512]{2,3,1,0:T(8,128)(2,1)S(1)}, bf16[2,3,128,512]{2,3,1,0:T(8,128)(2,1)}, u32[]{:S(2)}, u32[]{:S(2)}) collective-permute-start(bf16[2,3,128,512]{2,3,1,0:T(8,128)(2,1)S(1)} %get-tuple-element.236), channel_id=1, source_target_pairs={{0,4},{4,8},{8,12},{12,16},{16,20},{20,24},{24,28},{1,5},{5,9},{9,... | collective-permute-start | bytes 2359304 | tf_op jit(solution)/shard_map/ppermute | solution.py:31
  197.7 33.0 %collective-permute-start.3 = (bf16[2,3,128,512]{2,3,1,0:T(8,128)(2,1)S(1)}, bf16[2,3,128,512]{2,3,1,0:T(8,128)(2,1)}, u32[]{:S(2)}, u32[]{:S(2)}) collective-permute-start(bf16[2,3,128,512]{2,3,1,0:T(8,128)(2,1)S(1)} %get-tuple-element.237), channel_id=1, source_target_pairs={{4,0},{8,4},{12,8},{16,12},{20,16},{24,20},{28,24},{5,1},{9,5},{13... | collective-permute-start | bytes 2359304 | tf_op jit(solution)/shard_map/ppermute | solution.py:31
  233.0 5.1 %copy-start.1 = (bf16[1,3,128,512]{3,2,1,0:T(8,128)(2,1)}, bf16[1,3,128,512]{3,2,1,0:T(8,128)(2,1)S(1)}, u32[]{:S(2)}) copy-start(bf16[1,3,128,512]{3,2,1,0:T(8,128)(2,1)S(1)} %copy.91) | copy-start | bytes 1179652
  233.2 4.9 %copy-start.2 = (bf16[1,3,128,512]{3,2,1,0:T(8,128)(2,1)}, bf16[1,3,128,512]{3,2,1,0:T(8,128)(2,1)S(1)}, u32[]{:S(2)}) copy-start(bf16[1,3,128,512]{3,2,1,0:T(8,128)(2,1)S(1)} %copy.92) | copy-start | bytes 1179652
  238.1 4.8 %copy-start.12 = (u32[32]{0:T(128)S(1)}, u32[32]{0:T(128)}, u32[]{:S(2)}) copy-start(u32[32]{0:T(128)} %constant.190) | copy-start | bytes 388
  242.9 109.8 %all-reduce.9.cloned.1.call-start = ((), (), s32[]{:S(2)}) async-start(), calls=%async_computation.6 | async-start | bytes 1048576
  246.0 76.2 %copy-start.3 = (bf16[1,3,128,512]{3,2,1,0:T(8,128)(2,1)S(1)}, bf16[1,3,128,512]{3,2,1,0:T(8,128)(2,1)}, u32[]{:S(2)}) copy-start(bf16[1,3,128,512]{3,2,1,0:T(8,128)(2,1)} %copy-done.2) | copy-start | bytes 1179652
  320.2 50.0 %all-reduce.7.cloned.1.call-start = ((), (), s32[]{:S(2)}) async-start(), calls=%async_computation.4 | async-start | bytes 1572864 | tf_op jit(solution)/shard_map/psum | solution.py:149
  320.2 2.1 copy-start.7
Sparse Core Ops, SparseCore 0:
  9.6 23.9 all-gather.5
  35.1 21.2 all-gather.3
  58.0 21.2 all-gather.7
  243.0 74.6 reduce-scatter.3
  320.3 27.6 all-reduce.8
  350.9 19.2 all-reduce.6
where the time goes:
time: 381 us; the launch traced here: 379 us
  waiting for transfers between devices  189 us (50%)
  matrix products  56 us (15%)
  other arithmetic  43.8 us (11%)
  local copies, waits for them, and re-layouts  41.8 us (11%)
  loops' own time  19.7 us (5%)
  between operations  15.1 us (4%)
  starting transfers between devices  13.9 us (4%)
    unnamed x8, waiting for transfers between devices  73.8 us
    ppermute x2, waiting for transfers between devices, shifted(): lax.ppermute(value, axis, [(source, source + steps) for source in range(l...  29 us
    scatter-add x6, other arithmetic, backward(): running.at[0, slot_rows].add(key_part).at[1, slot_rows].add(value_part)  27.2 us
    all_gather x1, waiting for transfers between devices, per_device(): lax.all_gather(w_value, 'dp', axis=0, tiled=True)  24.1 us
    all_gather x1, waiting for transfers between devices, per_device(): lax.all_gather(w_key, 'dp', axis=0, tiled=True)  21.1 us
    psum x1, waiting for transfers between devices, per_device(): grad_input = lax.psum(partial_input.astype(jnp.bfloat16), 'section')[None]  15.5 us
    ppermute x1, waiting for transfers between devices, extended(): lax.ppermute(tail, axis, [(i, (i + 1) % count) for i in range(ends)])  14.1 us
    unnamed x34, local copies, waits for them, and re-layouts  12.8 us
  transfers between devices with their start and end apart: 10, of which 7 were waited for; matrix products, arithmetic and copies ran while one was open for 10% of the time, Pallas kernels for 0%

commit v1 on v0

--- a/solution.py
+++ b/solution.py
@@ -146,7 +146,9 @@
         + lax.dot_general(key_grad, key_full, contract, preferred_element_type=jnp.float32)
         + lax.dot_general(value_grad, value_full, contract, preferred_element_type=jnp.float32)
     )
-    grad_input = lax.psum(partial_input.astype(jnp.bfloat16), "section")[None]
+    grad_input = jnp.sum(lax.all_gather(partial_input.astype(jnp.bfloat16), "section"), axis=0)[
+        None
+    ]
     grads_all = jnp.stack([query_grad, key_grad, value_grad], axis=1)
     group_part = lax.psum_scatter(
         jnp.einsum("tr,tcf->rcf", tokens, grads_all, preferred_element_type=jnp.float32).astype(

time: 381 us -> 372 us (0.976)
  waiting for transfers between devices: 189 us -> 181 us
    psum x1 -> x0, waiting for transfers between devices: 15.5 us -> none  [per_device(): grad_input = lax.psum(partial_input.astype(jnp.bfloat16), 'section')[None]]
    unnamed x8, waiting for transfers between devices: 73.8 us -> 79.7 us
    unnamed x34 -> x27, local copies, waits for them, and re-layouts: 12.8 us -> 10.8 us
where the time goes in v1:
time: 372 us; the launch traced here: 371 us
  waiting for transfers between devices  181 us (49%)
  matrix products  54.8 us (15%)
  other arithmetic  46.5 us (12%)
  local copies, waits for them, and re-layouts  39.5 us (11%)
  loops' own time  19.7 us (5%)
  between operations  15.1 us (4%)
  starting transfers between devices  13.8 us (4%)
    unnamed x8, waiting for transfers between devices  79.7 us
    ppermute x2, waiting for transfers between devices, shifted(): lax.ppermute(value, axis, [(source, source + steps) for source in range(l...  31.1 us
    scatter-add x6, other arithmetic, backward(): running.at[0, slot_rows].add(key_part).at[1, slot_rows].add(value_part)  27.2 us
    all_gather x1, waiting for transfers between devices, per_device(): lax.all_gather(w_value, 'dp', axis=0, tiled=True)  24.1 us
    all_gather x1, waiting for transfers between devices, per_device(): lax.all_gather(w_key, 'dp', axis=0, tiled=True)  21.1 us
    ppermute x1, waiting for transfers between devices, extended(): lax.ppermute(tail, axis, [(i, (i + 1) % count) for i in range(ends)])  14.1 us
    dot_general x6, matrix products, attend(): jnp.einsum('qhd,skhd->hqsk', query_block, key_window, preferred_element_t...  12.4 us
    all_gather x1, waiting for transfers between devices, per_device(): lax.all_gather(w_query, 'dp', axis=0, tiled=True)  11.3 us
  transfers between devices with their start and end apart: 10, of which 7 were waited for; matrix products, arithmetic and copies ran while one was open for 10% of the time, Pallas kernels for 0%

profile of v1, /device:TPU:0, one launch (start us, length us, event | category | flops | bytes accessed | tf_op | source)
XLA Modules:
  0.0 370.7 jit_solution(15879130323404674931)
XLA Ops:
  9.5 24.1 %all-gather.8.cloned.1.call-done = bf16[1024,512]{1,0:T(8,128)(2,1)} async-done(((bf16[512,512]{1,0:T(8,128)(2,1)}), bf16[1024,512]{1,0:T(8,128)(2,1)}) %all-gather.8.cloned.1.call-update) | async-done | bytes 1048592 | tf_op jit(solution)/shard_map/all_gather | solution.py:59
  35.4 21.1 %all-gather.6.cloned.1.call-done = bf16[1024,512]{1,0:T(8,128)(2,1)} async-done(((bf16[512,512]{1,0:T(8,128)(2,1)}), bf16[1024,512]{1,0:T(8,128)(2,1)}) %all-gather.6.cloned.1.call-update) | async-done | bytes 1048592 | tf_op jit(solution)/shard_map/all_gather | solution.py:58
  60.4 5.4 %collective-permute-start = (bf16[2,384,512]{2,1,0:T(8,128)(2,1)S(1)}, bf16[2,384,512]{2,1,0:T(8,128)(2,1)}, u32[]{:S(2)}, u32[]{:S(2)}) collective-permute-start(bf16[2,384,512]{2,1,0:T(8,128)(2,1)S(1)} %pad_maximum_fusion.1), channel_id=1, source_target_pairs={{0,4},{4,8},{8,12},{12,16},{16,20},{20,24},{24,28},{1,5},{5,9},{9,... | collective-permute-start | bytes 2359304 | tf_op jit(solution)/shard_map/ppermute | solution.py:19
  68.1 11.3 %all-gather.10.cloned.1.call-done = bf16[1024,512]{1,0:T(8,128)(2,1)} async-done(((bf16[512,512]{1,0:T(8,128)(2,1)}), bf16[1024,512]{1,0:T(8,128)(2,1)}) %all-gather.10.cloned.1.call-update) | async-done | bytes 1048592 | tf_op jit(solution)/shard_map/all_gather | solution.py:57
  82.9 14.1 %collective-permute-done = bf16[2,384,512]{2,1,0:T(8,128)(2,1)} collective-permute-done((bf16[2,384,512]{2,1,0:T(8,128)(2,1)S(1)}, bf16[2,384,512]{2,1,0:T(8,128)(2,1)}, u32[]{:S(2)}, u32[]{:S(2)}) %collective-permute-start) | collective-permute-done | bytes 786464 | tf_op jit(solution)/shard_map/ppermute | solution.py:19
  98.8 4.6 %reshape.201 = bf16[2,9,128,8,64]{4,3,2,1,0:T(8,128)(2,1)} reshape(bf16[2,1152,512]{2,1,0:T(8,128)(2,1)S(1)} %pad_maximum_fusion) | data formatting | bytes 4718592 | tf_op jit(solution)/shard_map/reshape | solution.py:67
  103.3 6.1 %copy.83 = bf16[2,9,128,8,64]{2,4,1,3,0:T(8,128)(2,1)} copy(bf16[2,9,128,8,64]{4,3,2,1,0:T(8,128)(2,1)} %reshape.201) | data formatting | bytes 4718592 | tf_op jit(solution)/shard_map/while | solution.py:96
  109.5 2.8 broadcast_in_dim.61
  112.3 76.9 %while.27 = (s32[]{:T(128)}, f32[2,9,128,8,64]{2,4,3,1,0:T(8,128)}, bf16[3,128,8,64]{1,3,2,0:T(8,128)(2,1)S(1)}, s32[3]{0:T(128)S(1)}, s32[3,7]{1,0:T(4,128)S(1)...) while((s32[]{:T(128)}, f32[2,9,128,8,64]{2,4,3,1,0:T(8,128)}, ...), condition=%wide.region_10.11_spmd, body=%wide.region_4.10_spmd.sunk | while | flops 611644544 | bytes 56669256 | solution.py:128
  128.9 4.8 %scatter_fusion = f32[2,9,128,8,64]{2,4,3,1,0:T(8,128)} fusion(f32[2,9,128,8,64]{2,4,3,1,0:T(8,128)} %get-tuple-element.398, s32[7]{0:T(128)S(1)} %select_bitcast_fusion.5, f32[7,128,8,64]{1,3,2,0:T(8,128)} %copy.129), kind=kCustom, calls=%fused_computation.clone.1 | custom fusion | flops 458752 | bytes 5505080 | tf_op jit(solution)/shard_map/while/body/eval_jaxpr/scatter-add | solution.py:124
  133.7 4.3 %scatter_fusion.1 = f32[2,9,128,8,64]{2,4,3,1,0:T(8,128)} fusion(f32[2,9,128,8,64]{2,4,3,1,0:T(8,128)} %scatter_fusion, s32[7]{0:T(128)S(1)} %get-tuple-element.349, f32[7,128,8,64]{1,3,2,0:T(8,128)S(1)} %copy.130), kind=kCustom, calls=%fused_computation.1.clone.1 | custom fusion | flops 458752 | bytes 5505080 | tf_op jit(solution)/shard_map/while/body/eval_jaxpr/scatter-add | solution.py:124
  154.5 4.8 %scatter_fusion = f32[2,9,128,8,64]{2,4,3,1,0:T(8,128)} fusion(f32[2,9,128,8,64]{2,4,3,1,0:T(8,128)} %get-tuple-element.398, s32[7]{0:T(128)S(1)} %select_bitcast_fusion.5, f32[7,128,8,64]{1,3,2,0:T(8,128)} %copy.129), kind=kCustom, calls=%fused_computation.clone.1 | custom fusion | flops 458752 | bytes 5505080 | tf_op jit(solution)/shard_map/while/body/eval_jaxpr/scatter-add | solution.py:124
  159.4 4.2 %scatter_fusion.1 = f32[2,9,128,8,64]{2,4,3,1,0:T(8,128)} fusion(f32[2,9,128,8,64]{2,4,3,1,0:T(8,128)} %scatter_fusion, s32[7]{0:T(128)S(1)} %get-tuple-element.349, f32[7,128,8,64]{1,3,2,0:T(8,128)S(1)} %copy.130), kind=kCustom, calls=%fused_computation.1.clone.1 | custom fusion | flops 458752 | bytes 5505080 | tf_op jit(solution)/shard_map/while/body/eval_jaxpr/scatter-add | solution.py:124
  180.2 4.8 %scatter_fusion = f32[2,9,128,8,64]{2,4,3,1,0:T(8,128)} fusion(f32[2,9,128,8,64]{2,4,3,1,0:T(8,128)} %get-tuple-element.398, s32[7]{0:T(128)S(1)} %select_bitcast_fusion.5, f32[7,128,8,64]{1,3,2,0:T(8,128)} %copy.129), kind=kCustom, calls=%fused_computation.clone.1 | custom fusion | flops 458752 | bytes 5505080 | tf_op jit(solution)/shard_map/while/body/eval_jaxpr/scatter-add | solution.py:124
  185.0 4.2 %scatter_fusion.1 = f32[2,9,128,8,64]{2,4,3,1,0:T(8,128)} fusion(f32[2,9,128,8,64]{2,4,3,1,0:T(8,128)} %scatter_fusion, s32[7]{0:T(128)S(1)} %get-tuple-element.349, f32[7,128,8,64]{1,3,2,0:T(8,128)S(1)} %copy.130), kind=kCustom, calls=%fused_computation.1.clone.1 | custom fusion | flops 458752 | bytes 5505080 | tf_op jit(solution)/shard_map/while/body/eval_jaxpr/scatter-add | solution.py:124
  189.2 2.8 bitcast_convert_fusion
  193.0 5.4 %collective-permute-start.2 = (bf16[2,3,128,512]{2,3,1,0:T(8,128)(2,1)}, bf16[2,3,128,512]{2,3,1,0:T(8,128)(2,1)}, u32[]{:S(2)}, u32[]{:S(2)}) collective-permute-start(bf16[2,3,128,512]{2,3,1,0:T(8,128)(2,1)} %get-tuple-element.236), channel_id=1, source_target_pairs={{0,4},{4,8},{8,12},{12,16},{16,20},{20,24},{24,28},{1,5},{5,9},{9,... | collective-permute-start | bytes 2359304 | tf_op jit(solution)/shard_map/ppermute | solution.py:31
  200.6 31.1 %collective-permute-done.2 = bf16[2,3,128,512]{2,3,1,0:T(8,128)(2,1)} collective-permute-done((bf16[2,3,128,512]{2,3,1,0:T(8,128)(2,1)}, bf16[2,3,128,512]{2,3,1,0:T(8,128)(2,1)}, u32[]{:S(2)}, u32[]{:S(2)}) %collective-permute-start.2) | collective-permute-done | bytes 786464 | tf_op jit(solution)/shard_map/ppermute | solution.py:31
  235.3 4.5 %convolution_convert_fusion = bf16[3,512,1024]{2,1,0:T(8,128)(2,1)} fusion(bf16[384,1,512]{0,2,1:T(8,128)(2,1)} %copy.97, bf16[384,1,512]{0,2,1:T(8,128)(2,1)S(1)} %copy.96, bf16[384,1,512]{0,2,1:T(8,128)(2,1)S(1)} %stack_reshape.3, bf16[1,384,1024]{2,1,0:T(8,128)(2,1)S(1)} %copy-done), kind=kOutput, calls=%fused_computation.64 | convolution fusion | flops 1210712064 | bytes 5111808 | tf_op jit(solution)/shard_map/tr,tcf->rcf/dot_general | solution.py:154
  239.8 4.7 %copy.120 = bf16[1024,1536]{1,0:T(8,128)(2,1)} copy(bf16[1024,1536]{0,1:T(8,128)(2,1)} %bitcast.204) | data formatting | bytes 6291456
  250.1 68.9 %reduce-scatter.4.cloned.1.call-done = bf16[128,1536]{1,0:T(8,128)(2,1)} async-done(((bf16[1024,1536]{1,0:T(8,128)(2,1)}), bf16[128,1536]{1,0:T(8,128)(2,1)}) %reduce-scatter.4.cloned.1.call-update) | async-done | bytes 393232
  321.5 27.2 %while.26 = (s32[]{:T(128)}, bf16[3,128,8,64]{1,3,2,0:T(8,128)(2,1)S(1)}, s32[3]{0:T(128)S(1)}, bf16[2,9,128,8,64]{2,4,1,3,0:T(8,128)(2,1)}, s32[3,7]{1,0:T(4,12...) while((s32[]{:T(128)}, ...), condition=%wide.region_3.4_spmd, body=%wide.region_0.3_spmd.sunk | while | flops 245954576 | bytes 13128970 | solution.py:96
  350.4 2.9 reduce_sum.39
  353.2 8.7 %all-reduce.6.cloned.1.call-done = bf16[128,3,512]{2,1,0:T(4,128)(2,1)} async-done(((bf16[128,3,512]{2,1,0:T(4,128)(2,1)}), bf16[128,3,512]{2,1,0:T(4,128)(2,1)}) %all-reduce.6.cloned.1.call-update) | async-done | bytes 393232
  (125 shorter events, 90.4 us)
Async XLA Ops:
  7.2 26.4 %copy-start = (bf16[1,384,1024]{2,1,0:T(8,128)(2,1)S(1)}, bf16[1,384,1024]{2,1,0:T(8,128)(2,1)}, u32[]{:S(2)}) copy-start(bf16[1,384,1024]{2,1,0:T(8,128)(2,1)} %param.18) | copy-start | bytes 2359300
  7.2 26.4 %all-gather.8.cloned.1.call-start = ((), (), s32[]{:S(2)}) async-start(), calls=%async_computation.2 | async-start | bytes 1572864 | tf_op jit(solution)/shard_map/all_gather | solution.py:59
  7.9 48.6 %all-gather.6.cloned.1.call-start = ((), (), s32[]{:S(2)}) async-start(), calls=%async_computation.1 | async-start | bytes 1572864 | tf_op jit(solution)/shard_map/all_gather | solution.py:58
  8.7 57.2 %copy-start.7 = (s32[24,7]{0,1:T(8,128)S(1)}, s32[24,7]{0,1:T(8,128)}, u32[]{:S(2)}) copy-start(s32[24,7]{0,1:T(8,128)} %param.22) | copy-start | bytes 2020
  8.7 57.3 %copy-start.6 = (bf16[1,384,512]{2,1,0:T(8,128)(2,1)S(1)}, bf16[1,384,512]{2,1,0:T(8,128)(2,1)}, u32[]{:S(2)}) copy-start(bf16[1,384,512]{2,1,0:T(8,128)(2,1)} %param.23) | copy-start | bytes 1179652
  8.7 70.7 %all-gather.10.cloned.1.call-start = ((), (), s32[]{:S(2)}) async-start(), calls=%async_computation.3 | async-start | bytes 1572864 | tf_op jit(solution)/shard_map/all_gather | solution.py:57
  9.4 309.6 %reduce-scatter.4.cloned.1.call-start = ((), (), s32[]{:S(2)}) async-start(), calls=%async_computation.5 | async-start | bytes 3538944
  35.4 30.4 %copy-start.1 = (bf16[1,384,512]{2,1,0:T(8,128)(2,1)}, bf16[1,384,512]{2,1,0:T(8,128)(2,1)S(1)}, u32[]{:S(2)}) copy-start(bf16[1,384,512]{2,1,0:T(8,128)(2,1)S(1)} %fusion.43) | copy-start | bytes 1179652
  58.3 0.7 copy-start.2
  59.1 22.9 %collective-permute-start.1 = (bf16[2,384,512]{2,1,0:T(8,128)(2,1)S(1)}, bf16[2,384,512]{2,1,0:T(8,128)(2,1)S(1)}, u32[]{:S(2)}, u32[]{:S(2)}) collective-permute-start(bf16[2,384,512]{2,1,0:T(8,128)(2,1)S(1)} %pad_maximum_fusion.1), channel_id=1, source_target_pairs={{4,0},{8,4},{12,8},{16,12},{20,16},{24,20},{28,24},{5,1},{9,5},{13... | collective-permute-start | bytes 2359304 | tf_op jit(solution)/shard_map/ppermute | solution.py:21
  60.4 36.6 %collective-permute-start = (bf16[2,384,512]{2,1,0:T(8,128)(2,1)S(1)}, bf16[2,384,512]{2,1,0:T(8,128)(2,1)}, u32[]{:S(2)}, u32[]{:S(2)}) collective-permute-start(bf16[2,384,512]{2,1,0:T(8,128)(2,1)S(1)} %pad_maximum_fusion.1), channel_id=1, source_target_pairs={{0,4},{4,8},{8,12},{12,16},{16,20},{20,24},{24,28},{1,5},{5,9},{9,... | collective-permute-start | bytes 2359304 | tf_op jit(solution)/shard_map/ppermute | solution.py:19
  82.1 0.9 copy-start.5
  109.5 2.9 copy-start.8
  193.0 38.6 %collective-permute-start.2 = (bf16[2,3,128,512]{2,3,1,0:T(8,128)(2,1)}, bf16[2,3,128,512]{2,3,1,0:T(8,128)(2,1)}, u32[]{:S(2)}, u32[]{:S(2)}) collective-permute-start(bf16[2,3,128,512]{2,3,1,0:T(8,128)(2,1)} %get-tuple-element.236), channel_id=1, source_target_pairs={{0,4},{4,8},{8,12},{12,16},{16,20},{20,24},{24,28},{1,5},{5,9},{9,... | collective-permute-start | bytes 2359304 | tf_op jit(solution)/shard_map/ppermute | solution.py:31
  198.4 33.3 %collective-permute-start.3 = (bf16[2,3,128,512]{2,3,1,0:T(8,128)(2,1)S(1)}, bf16[2,3,128,512]{2,3,1,0:T(8,128)(2,1)}, u32[]{:S(2)}, u32[]{:S(2)}) collective-permute-start(bf16[2,3,128,512]{2,3,1,0:T(8,128)(2,1)S(1)} %get-tuple-element.237), channel_id=1, source_target_pairs={{4,0},{8,4},{12,8},{16,12},{20,16},{24,20},{28,24},{5,1},{9,5},{13... | collective-permute-start | bytes 2359304 | tf_op jit(solution)/shard_map/ppermute | solution.py:31
  244.5 2.1 copy-start.3
  244.5 105.8 %all-gather.12.cloned.1.call-start = ((), (), s32[]{:S(2)}) async-start(), calls=%async_computation.4 | async-start | bytes 2359296 | tf_op jit(solution)/shard_map/all_gather | solution.py:149
  244.6 2.6 copy-start.4
  247.2 1.6 copy-start.9
  248.8 113.1 %all-reduce.6.cloned.1.call-start = ((), (), s32[]{:S(2)}) async-start(), calls=%async_computation.6 | async-start | bytes 1048576
Sparse Core Ops, SparseCore 0:
  9.6 23.9 all-gather.7
  35.1 21.2 all-gather.5
  58.0 21.2 all-gather.9
  244.7 74.2 reduce-scatter.3
  321.0 8.9 all-gather.11
  332.1 29.7 all-reduce.5
